TPU v7x, 512 devices: a whole 4x4x16 slice. The times are simulated.
512 devices in a mesh: dp: 32 (over x, y, core), expert: 16 (over z).
Axes of the slice: x: 4, y: 4, z: 16, core: 2. Of those that a mesh axis runs over, the one named last changes fastest.
Arguments:
- out_grad: bfloat16 [65536, 2048], P(('dp', 'expert')), may hold values from -6 to 6
- expert_ids: int32 [65536, 4], P(('dp', 'expert')), may hold values from 0 to 15, all different within a row; in each aligned block of 128 rows (0 to 127, 128 to 255, ...) at most 64 rows name the same one
- route_weights: bfloat16 [65536, 4], P(('dp', 'expert')), may hold values from 0.049804688 to 1
- pre_activations: bfloat16 [65536, 4, 1536], P(('dp', 'expert')), may hold values from -6 to 6
- down_weight: bfloat16 [16, 768, 2048], P('expert', 'dp'), may hold values from -0.21875 to 0.21875
Outputs:
- pre_grad: bfloat16 [65536, 4, 1536], P(('dp', 'expert'))
- weight_grad: bfloat16 [65536, 4], P(('dp', 'expert'))
- down_grad: bfloat16 [16, 768, 2048], P('expert', 'dp')
Inputs may be any that keep to these rules, and one draw needn't show every extreme that they name: `expert_ids`: among the 128 rows of one device, each expert is named by at most 64 rows, a bound that some block reaches; the numbers in a row are distinct.
All inputs are finite; a program needn't handle non-finite values.
Results may differ from a plain program's by a relative error of at most 0.015.
Values may be sent and summed in bfloat16 or wider, within the bound.
No kernel may reach another device: no remote copies, remote signals or barrier semaphores. Data moves between devices by JAX's collectives and lax.ppermute only.
A program may use at most 64 MiB of HBM per device.

v0:
```python
import jax
import jax.numpy as jnp
from jax import lax
from jax.sharding import PartitionSpec as P

F32 = jnp.float32
BF16 = jnp.bfloat16


def gather_rows(x):
    return lax.all_gather(x, "dp", axis=0, tiled=True)


def body(out_grad, expert_ids, route_weights, pre_activations, down_weight):
    tok, width = out_grad.shape
    top = expert_ids.shape[1]
    units = pre_activations.shape[2] // 2
    ndp = lax.axis_size("dp")
    rows = down_weight.shape[1]
    n_all = ndp * tok
    w_all = lax.all_gather(down_weight, "expert", axis=0, tiled=True)
    experts = w_all.shape[0]
    wcat = w_all.reshape(experts * rows, width)
    og_all = gather_rows(out_grad)
    ids_t = gather_rows(expert_ids).T
    rw_t = gather_rows(route_weights).T.astype(F32)
    gate = pre_activations[..., :units].astype(F32)
    up = pre_activations[..., units:].astype(F32)
    sig = jax.nn.sigmoid(gate)
    hidden = (gate * sig * up).astype(BF16)
    send_h = hidden.reshape(tok, top, ndp, rows).transpose(2, 0, 1, 3)
    got_h = lax.all_to_all(send_h, "dp", 0, 0, tiled=True)
    hid_t = got_h.transpose(2, 3, 0, 1).reshape(top, rows, n_all).astype(F32)
    eidx = jnp.arange(experts, dtype=jnp.int32)[:, None, None]
    hp = jnp.zeros((experts, rows, n_all), F32)
    for k in range(top):
        hp = hp + jnp.where(
            ids_t[k][None, None, :] == eidx, (rw_t[k][None, :] * hid_t[k])[None], 0.0
        )
    hp = hp.reshape(experts * rows, n_all).astype(BF16)
    part = lax.dot_general(hp, og_all, (((1,), (0,)), ((), ())), preferred_element_type=F32)
    r_t = lax.dot_general(wcat, og_all, (((1,), (1,)), ((), ())), preferred_element_type=F32)
    r_t = r_t.reshape(experts, rows, n_all)
    hg_t = jnp.stack(
        [jnp.sum(jnp.where(ids_t[k][None, None, :] == eidx, r_t, 0.0), axis=0) for k in range(top)]
    ).astype(BF16)
    send_g = hg_t.reshape(top, rows, ndp, tok).transpose(2, 3, 0, 1)
    got_g = lax.all_to_all(send_g, "dp", 0, 0, tiled=True)
    hidden_grad = got_g.transpose(1, 2, 0, 3).reshape(tok, top, units)
    hg32 = hidden_grad.astype(F32)
    weight_grad = jnp.sum(hg32 * hidden.astype(F32), axis=-1).astype(BF16)
    cot = route_weights.astype(F32)[..., None] * hg32
    gate_grad = cot * up * sig * (1.0 + gate * (1.0 - sig))
    up_grad = cot * gate * sig
    pre_grad = jnp.concatenate([gate_grad, up_grad], axis=-1).astype(BF16)
    summed = lax.psum_scatter(
        part.reshape(experts, rows, width).astype(BF16), "expert", scatter_dimension=0, tiled=True
    )
    down_grad = (summed.astype(F32) / ndp).astype(BF16)
    return (pre_grad, weight_grad, down_grad)


def solution(mesh):
    return jax.shard_map(
        body,
        mesh=mesh,
        in_specs=(
            P(("dp", "expert"), None),
            P(("dp", "expert"), None),
            P(("dp", "expert"), None),
            P(("dp", "expert"), None, None),
            P("expert", "dp", None),
        ),
        out_specs=(
            P(("dp", "expert"), None, None),
            P(("dp", "expert"), None),
            P("expert", "dp", None),
        ),
        check_vma=False,
    )
```

profile of v0, /device:TPU:4, one launch (start us, length us, event | category | flops | bytes accessed | tf_op | source)
XLA Modules:
  0.0 325.2 jit_solution(932634305599170821)
XLA Ops:
  7.2 0.0 all-gather.3.cloned.1.call-start
  7.2 0.7 all-gather.3.cloned.1.call-update
  7.9 0.0 all-gather.5.cloned.1.call-start
  7.9 0.7 all-gather.5.cloned.1.call-update
  8.6 1.9 fusion.30
  10.6 0.0 copy-start.1
  10.6 0.0 copy-start.2
  10.6 0.7 copy.37
  11.3 0.7 copy.36
  11.9 0.0 copy-done.1
  12.0 24.4 %all_gather.15 = bf16[4096,4]{0,1:T(4,128)(2,1)S(1)} all-gather(bf16[128,4]{0,1:T(4,128)(2,1)S(1)} %copy-done.1), channel_id=1, replica_groups=mesh['dp'=32,'expert'=16] {'dp'}, dimensions={0}, use_global_device_ids=true | all-gather | bytes 33792 | tf_op jit(solution)/shard_map/all_gather | solution.py:11
  36.4 0.0 copy-done.2
  36.4 24.9 %all_gather.12 = s32[4096,4]{0,1:T(4,128)S(1)} all-gather(s32[128,4]{0,1:T(4,128)S(1)} %copy-done.2), channel_id=1, replica_groups=mesh['dp'=32,'expert'=16] {'dp'}, dimensions={0}, use_global_device_ids=true | all-gather | bytes 67584 | tf_op jit(solution)/shard_map/all_gather | solution.py:11
  61.4 0.1 iota_compare_fusion.2
  61.5 0.1 iota_compare_fusion
  61.5 24.7 %all-gather.3.cloned.1.call-done = bf16[16,24,2048]{2,1,0:T(8,128)(2,1)} async-done(((bf16[1,24,2048]{2,1,0:T(8,128)(2,1)}), bf16[16,24,2048]{2,1,0:T(8,128)(2,1)}) %all-gather.3.cloned.1.call-update) | async-done | bytes 1572880 | tf_op jit(solution)/shard_map/all_gather | solution.py:21
  86.3 88.2 %all-gather.5.cloned.1.call-done = bf16[4096,2048]{1,0:T(8,128)(2,1)} async-done(((bf16[128,2048]{1,0:T(8,128)(2,1)}), bf16[4096,2048]{1,0:T(8,128)(2,1)}) %all-gather.5.cloned.1.call-update) | async-done | bytes 16777232 | tf_op jit(solution)/shard_map/all_gather | solution.py:11
  174.5 12.7 %select_reduce_fusion.3 = (bf16[24,4096]{1,0:T(8,128)(2,1)S(1)}, bf16[24,4096]{1,0:T(8,128)(2,1)S(1)}, bf16[24,4096]{1,0:T(8,128)(2,1)S(1)}, bf16[24,4096]{1,0:T(8,128)(2,1)S(1)}) fusion(pred[16,4096]{1,0:T(8,128)(4,1)S(1)} %get-tuple-element.37, pred[16,4096]{1,0:T(8,128)(4,1)S(1)} %get-tuple-element.34, pred[16,4096]{1,0:T(8,128)(4,1)S(1)} %get-tuple-element.35, ...), kind=kOutput, calls=%fused_computation.8 | convolution fusion | flops 6454640640 | bytes 19398656 | tf_op jit(solution)/shard_map/dot_general | solution.py:42
  187.4 0.1 maximum_bitcast_fusion
  187.5 1.2 copy.25
  188.7 5.7 %all-to-all-start = ((bf16[32,128,4,24]{1,3,2,0:T(8,128)(2,1)}), bf16[32,128,4,24]{1,3,2,0:T(8,128)(2,1)S(1)}, u32[]{:S(2)}, u32[]{:S(2)}) async-start(bf16[32,128,4,24]{1,3,2,0:T(8,128)(2,1)} %copy.25), calls=%async_computation | async-start | bytes 1572864 | tf_op jit(solution)/shard_map/all_to_all | solution.py:48
  194.4 12.1 %all-to-all-done = bf16[32,128,4,24]{1,3,2,0:T(8,128)(2,1)S(1)} async-done(((bf16[32,128,4,24]{1,3,2,0:T(8,128)(2,1)}), bf16[32,128,4,24]{1,3,2,0:T(8,128)(2,1)S(1)}, u32[]{:S(2)}, u32[]{:S(2)}) %all-to-all-start) | async-done | bytes 786464 | tf_op jit(solution)/shard_map/all_to_all | solution.py:48
  206.5 2.6 fusion.26
  209.1 1.0 copy.29
  210.1 5.9 %all-to-all-start.1 = ((bf16[32,128,4,24]{1,3,2,0:T(8,128)(2,1)}), bf16[32,128,4,24]{1,3,2,0:T(8,128)(2,1)S(1)}, u32[]{:S(2)}, u32[]{:S(2)}) async-start(bf16[32,128,4,24]{1,3,2,0:T(8,128)(2,1)} %copy.29), calls=%async_computation.1 | async-start | bytes 1572864 | tf_op jit(solution)/shard_map/all_to_all | solution.py:32
  216.0 0.2 reduce-scatter.2.cloned.1.call-start
  216.3 11.8 %all-to-all-done.1 = bf16[32,128,4,24]{1,3,2,0:T(8,128)(2,1)S(1)} async-done(((bf16[32,128,4,24]{1,3,2,0:T(8,128)(2,1)}), bf16[32,128,4,24]{1,3,2,0:T(8,128)(2,1)S(1)}, u32[]{:S(2)}, u32[]{:S(2)}) %all-to-all-start.1) | async-done | bytes 786464 | tf_op jit(solution)/shard_map/all_to_all | solution.py:32
  228.1 0.3 convert_bitcast_fusion
  228.4 0.1 fusion.29
  228.5 0.3 broadcast_multiply_fusion
  228.8 0.2 copy.50
  229.1 0.3 broadcast_multiply_fusion.1
  229.4 0.2 copy.51
  229.6 0.3 broadcast_multiply_fusion.2
  229.9 0.2 copy.52
  230.2 0.3 broadcast_multiply_fusion.3
  230.5 0.2 copy.53
  230.8 13.7 %fusion.13 = bf16[16,24,2048]{2,1,0:T(8,128)(2,1)} fusion(bf16[4096,2048]{1,0:T(8,128)(2,1)} %all-gather.5.cloned.1.call-done, f32[24,4096]{1,0:T(8,128)S(1)} %bitcast.84, f32[24,4096]{1,0:T(8,128)S(1)} %bitcast.85, f32[24,4096]{1,0:T(8,128)S(1)} %bitcast.86, f32[24,4096]{1,0:T(8,128)S(1)} %bitcast.87, pred[16,4096]{1,0:T(8,128)(4,1)S(1)} %get-tuple-element.34, ...), kind=kOutput, calls=%fused_computation.18 | convolution fusion | flops 6455820288 | bytes 20185088 | tf_op jit(solution)/shard_map/dot_general | solution.py:41
  244.4 0.0 copy-start
  244.4 0.0 reduce-scatter.2.cloned.1.call-update
  244.5 1.1 copy-done
  245.6 0.1 pad_maximum_fusion
  245.7 2.5 copy.31
  248.2 69.0 %reduce-scatter.2.cloned.1.call-done = bf16[1,24,2048]{2,1,0:T(8,128)(2,1)} async-done(((bf16[16,24,2048]{2,1,0:T(8,128)(2,1)}), bf16[1,24,2048]{2,1,0:T(8,128)(2,1)}) %reduce-scatter.2.cloned.1.call-update) | async-done | bytes 98320 | tf_op jit(solution)/shard_map/reduce_scatter | solution.py:56
  317.1 1.6 multiply_convert_fusion
  (8 shorter events, 0.2 us)
Async XLA Ops:
  7.2 79.1 %all-gather.3.cloned.1.call-start = ((), (), s32[]{:S(2)}) async-start(), calls=%async_computation.3 | async-start | bytes 1671168 | tf_op jit(solution)/shard_map/all_gather | solution.py:21
  7.9 166.6 %all-gather.5.cloned.1.call-start = ((), (), s32[]{:S(2)}) async-start(), calls=%async_computation.4 | async-start | bytes 17301504 | tf_op jit(solution)/shard_map/all_gather | solution.py:11
  10.6 1.4 copy-start.1
  10.6 25.8 %copy-start.2 = (s32[128,4]{0,1:T(4,128)S(1)}, s32[128,4]{0,1:T(4,128)}, u32[]{:S(2)}) copy-start(s32[128,4]{0,1:T(4,128)} %param.6) | copy-start | bytes 6148
  188.7 17.8 %all-to-all-start = ((bf16[32,128,4,24]{1,3,2,0:T(8,128)(2,1)}), bf16[32,128,4,24]{1,3,2,0:T(8,128)(2,1)S(1)}, u32[]{:S(2)}, u32[]{:S(2)}) async-start(bf16[32,128,4,24]{1,3,2,0:T(8,128)(2,1)} %copy.25), calls=%async_computation | async-start | bytes 1572864 | tf_op jit(solution)/shard_map/all_to_all | solution.py:48
  210.1 18.0 %all-to-all-start.1 = ((bf16[32,128,4,24]{1,3,2,0:T(8,128)(2,1)}), bf16[32,128,4,24]{1,3,2,0:T(8,128)(2,1)S(1)}, u32[]{:S(2)}, u32[]{:S(2)}) async-start(bf16[32,128,4,24]{1,3,2,0:T(8,128)(2,1)} %copy.29), calls=%async_computation.1 | async-start | bytes 1572864 | tf_op jit(solution)/shard_map/all_to_all | solution.py:32
  216.0 101.1 %reduce-scatter.2.cloned.1.call-start = ((), (), s32[]{:S(2)}) async-start(), calls=%async_computation.5 | async-start | bytes 1671168 | tf_op jit(solution)/shard_map/reduce_scatter | solution.py:56
  244.4 1.1 copy-start
Sparse Core Ops, SparseCore 0:
  10.1 76.1 all-gather.2
  89.4 85.0 all-gather.4
  244.6 72.4 reduce-scatter.1
where the time goes:
time: 326 us; the launch traced here: 325 us
  waiting for transfers between devices  207 us (63%)
  blocking collectives  49.4 us (15%)
  matrix products  26.4 us (8%)
  between operations  14 us (4%)
  starting transfers between devices  11.9 us (4%)
  local copies, waits for them, and re-layouts  10.3 us (3%)
  other arithmetic  6.07 us (2%)
    all_gather x1, waiting for transfers between devices, gather_rows(): return lax.all_gather(x, 'dp', axis=0, tiled=True)  88.2 us
    reduce_scatter x1, waiting for transfers between devices, body(): lax.psum_scatter(part.reshape(experts, rows, width).astype(BF16), 'expert...  69 us
    all_gather x2, blocking collectives, gather_rows(): return lax.all_gather(x, 'dp', axis=0, tiled=True)  49.4 us
    all_gather x1, waiting for transfers between devices, body(): w_all = lax.all_gather(down_weight, 'expert', axis=0, tiled=True)  24.7 us
    dot_general x1, matrix products, body(): lax.dot_general(hp, og_all, (((1,), (0,)), ((), ())), preferred_element_t...  13.7 us
    dot_general x1, matrix products, body(): lax.dot_general(wcat, og_all, (((1,), (1,)), ((), ())), preferred_element...  12.7 us
    all_to_all x1, waiting for transfers between devices, body(): got_g = lax.all_to_all(send_g, 'dp', 0, 0, tiled=True)  12.1 us
    all_to_all x1, waiting for transfers between devices, body(): got_h = lax.all_to_all(send_h, 'dp', 0, 0, tiled=True)  11.8 us
  transfers between devices with their start and end apart: 5, of which 5 were waited for; matrix products, arithmetic and copies ran while one was open for 2% of the time, Pallas kernels for 0%

commit v1 on v0

--- a/solution.py
+++ b/solution.py
@@ -5,6 +5,13 @@
 
 F32 = jnp.float32
 BF16 = jnp.bfloat16
+
+
+def divide_samples(my_tile, device_axis, dim_k):
+    p_next = lax.all_to_all(
+        jnp.stack([my_tile for _ in range(lax.axis_size(device_axis))]), device_axis, 0, 0
+    )
+    return jnp.concatenate(p_next, dim_k)
 
 
 def gather_rows(x):
@@ -18,7 +25,7 @@
     ndp = lax.axis_size("dp")
     rows = down_weight.shape[1]
     n_all = ndp * tok
-    w_all = lax.all_gather(down_weight, "expert", axis=0, tiled=True)
+    w_all = divide_samples(down_weight, "expert", 0)
     experts = w_all.shape[0]
     wcat = w_all.reshape(experts * rows, width)
     og_all = gather_rows(out_grad)

time: 326 us -> 255 us (0.78)
  waiting for transfers between devices: 207 us -> 121 us
  starting transfers between devices: 11.9 us -> 27.1 us
    all_gather x1, waiting for transfers between devices: 88.2 us -> 3.93 us  [gather_rows(): return lax.all_gather(x, 'dp', axis=0, tiled=True)]
    all_gather x1 -> x0, waiting for transfers between devices: 24.7 us -> none  [body(): w_all = lax.all_gather(down_weight, 'expert', axis=0, tiled=True)]
    all_to_all x0 -> x1, waiting for transfers between devices: none -> 23.6 us  [divide_samples(): lax.all_to_all(jnp.stack([my_tile for _ in range(lax.axis_size(device_axi...]
    all_to_all x0 -> x1, starting transfers between devices: none -> 15.2 us  [divide_samples(): lax.all_to_all(jnp.stack([my_tile for _ in range(lax.axis_size(device_axi...]
  transfers between devices with their start and end apart: 5 -> 5, of which waited for: 5 -> 5; matrix products, arithmetic and copies ran while one was open for 2% -> 3% of each run, Pallas kernels for 0% -> 0%
where the time goes in v1:
time: 255 us
  waiting for transfers between devices  121 us (47%)
  blocking collectives  47.2 us (19%)
  starting transfers between devices  27.1 us (11%)
  matrix products  26.4 us (10%)
  between operations  14.3 us (6%)
  local copies, waits for them, and re-layouts  12.5 us (5%)
  other arithmetic  6.07 us (2%)
    reduce_scatter x1, waiting for transfers between devices, body(): lax.psum_scatter(part.reshape(experts, rows, width).astype(BF16), 'expert...  69 us
    all_gather x2, blocking collectives, gather_rows(): return lax.all_gather(x, 'dp', axis=0, tiled=True)  47.2 us
    all_to_all x1, waiting for transfers between devices, divide_samples(): lax.all_to_all(jnp.stack([my_tile for _ in range(lax.axis_size(device_axi...  23.6 us
    all_to_all x1, starting transfers between devices, divide_samples(): lax.all_to_all(jnp.stack([my_tile for _ in range(lax.axis_size(device_axi...  15.2 us
    dot_general x1, matrix products, body(): lax.dot_general(hp, og_all, (((1,), (0,)), ((), ())), preferred_element_t...  13.6 us
    dot_general x1, matrix products, body(): lax.dot_general(wcat, og_all, (((1,), (1,)), ((), ())), preferred_element...  12.7 us
    all_to_all x1, waiting for transfers between devices, body(): got_g = lax.all_to_all(send_g, 'dp', 0, 0, tiled=True)  12.1 us
    all_to_all x1, waiting for transfers between devices, body(): got_h = lax.all_to_all(send_h, 'dp', 0, 0, tiled=True)  11.8 us
  transfers between devices with their start and end apart: 5, of which 5 were waited for; matrix products, arithmetic and copies ran while one was open for 3% of the time, Pallas kernels for 0%

profile of v1, /device:TPU:4, one launch (start us, length us, event | category | flops | bytes accessed | tf_op | source)
XLA Modules:
  0.0 254.6 jit_solution(1721709328803460538)
XLA Ops:
  7.2 0.0 all-gather.2.cloned.1.call-start
  7.2 0.7 all-gather.2.cloned.1.call-update
  7.9 2.2 stack.12
  10.1 15.2 %all-to-all-start = ((bf16[16,1,24,2048]{3,2,1,0:T(8,128)(2,1)}), bf16[16,1,24,2048]{3,2,1,0:T(8,128)(2,1)}, u32[]{:S(2)}, u32[]{:S(2)}) async-start(bf16[16,1,24,2048]{3,2,1,0:T(8,128)(2,1)} %stack.12), calls=%async_computation | async-start | bytes 3145728 | tf_op jit(solution)/shard_map/all_to_all | solution.py:11
  25.4 1.9 fusion.31
  27.3 0.0 copy-start.1
  27.3 0.0 copy-start.2
  27.3 0.7 copy.37
  28.0 0.7 copy.36
  28.7 0.0 copy-done.1
  28.7 23.1 %all_gather.11 = bf16[4096,4]{0,1:T(4,128)(2,1)S(1)} all-gather(bf16[128,4]{0,1:T(4,128)(2,1)S(1)} %copy-done.1), channel_id=1, replica_groups=mesh['dp'=32,'expert'=16] {'dp'}, dimensions={0}, use_global_device_ids=true | all-gather | bytes 33792 | tf_op jit(solution)/shard_map/all_gather | solution.py:18
  51.8 0.0 copy-done.2
  51.8 24.0 %all_gather.9 = s32[4096,4]{0,1:T(4,128)S(1)} all-gather(s32[128,4]{0,1:T(4,128)S(1)} %copy-done.2), channel_id=1, replica_groups=mesh['dp'=32,'expert'=16] {'dp'}, dimensions={0}, use_global_device_ids=true | all-gather | bytes 67584 | tf_op jit(solution)/shard_map/all_gather | solution.py:18
  75.9 0.1 iota_compare_fusion.2
  76.0 0.1 iota_compare_fusion
  76.1 23.6 %all-to-all-done = bf16[16,1,24,2048]{3,2,1,0:T(8,128)(2,1)} async-done(((bf16[16,1,24,2048]{3,2,1,0:T(8,128)(2,1)}), bf16[16,1,24,2048]{3,2,1,0:T(8,128)(2,1)}, u32[]{:S(2)}, u32[]{:S(2)}) %all-to-all-start) | async-done | bytes 1572896 | tf_op jit(solution)/shard_map/all_to_all | solution.py:11
  99.7 3.9 %all-gather.2.cloned.1.call-done = bf16[4096,2048]{1,0:T(8,128)(2,1)} async-done(((bf16[128,2048]{1,0:T(8,128)(2,1)}), bf16[4096,2048]{1,0:T(8,128)(2,1)}) %all-gather.2.cloned.1.call-update) | async-done | bytes 16777232 | tf_op jit(solution)/shard_map/all_gather | solution.py:18
  103.6 12.7 %select_reduce_fusion.3 = (bf16[24,4096]{1,0:T(8,128)(2,1)S(1)}, bf16[24,4096]{1,0:T(8,128)(2,1)S(1)}, bf16[24,4096]{1,0:T(8,128)(2,1)S(1)}, bf16[24,4096]{1,0:T(8,128)(2,1)S(1)}) fusion(pred[16,4096]{1,0:T(8,128)(4,1)S(1)} %get-tuple-element.37, pred[16,4096]{1,0:T(8,128)(4,1)S(1)} %get-tuple-element.34, pred[16,4096]{1,0:T(8,128)(4,1)S(1)} %get-tuple-element.35, ...), kind=kOutput, calls=%fused_computation.8 | convolution fusion | flops 6454640640 | bytes 19398656 | tf_op jit(solution)/shard_map/dot_general | solution.py:49
  116.5 0.1 maximum_bitcast_fusion
  116.6 1.2 copy.25
  117.8 5.7 %all-to-all-start.1 = ((bf16[32,128,4,24]{1,3,2,0:T(8,128)(2,1)}), bf16[32,128,4,24]{1,3,2,0:T(8,128)(2,1)S(1)}, u32[]{:S(2)}, u32[]{:S(2)}) async-start(bf16[32,128,4,24]{1,3,2,0:T(8,128)(2,1)} %copy.25), calls=%async_computation.1 | async-start | bytes 1572864 | tf_op jit(solution)/shard_map/all_to_all | solution.py:55
  123.5 12.1 %all-to-all-done.1 = bf16[32,128,4,24]{1,3,2,0:T(8,128)(2,1)S(1)} async-done(((bf16[32,128,4,24]{1,3,2,0:T(8,128)(2,1)}), bf16[32,128,4,24]{1,3,2,0:T(8,128)(2,1)S(1)}, u32[]{:S(2)}, u32[]{:S(2)}) %all-to-all-start.1) | async-done | bytes 786464 | tf_op jit(solution)/shard_map/all_to_all | solution.py:55
  135.6 2.6 %fusion.26 = (bf16[128,4]{0,1:T(4,128)(2,1)}, bf16[128,4,768]{0,2,1:T(8,128)(2,1)S(1)}, bf16[128,4,768]{0,2,1:T(8,128)(2,1)S(1)}, bf16[128,4,768]{0,2,1:T(8,128)(2,1)}) fusion(bf16[32,128,4,24]{1,3,2,0:T(8,128)(2,1)S(1)} %all-to-all-done.1, bf16[128,4,768]{0,2,1:T(8,128)(2,1)S(1)} %copy.37, bf16[128,4,768]{0,2,1:T(8,128)(2,1)S(1)} %copy.36, ...), kind=kLoop, calls=%fused_computation.38 | loop fusion | flops 9043456 | bytes 4721664 | tf_op jit(solution)/shard_map/reduce_sum | solution.py:58
  138.2 1.0 copy.29
  139.2 5.9 %all-to-all-start.2 = ((bf16[32,128,4,24]{1,3,2,0:T(8,128)(2,1)}), bf16[32,128,4,24]{1,3,2,0:T(8,128)(2,1)S(1)}, u32[]{:S(2)}, u32[]{:S(2)}) async-start(bf16[32,128,4,24]{1,3,2,0:T(8,128)(2,1)} %copy.29), calls=%async_computation.2 | async-start | bytes 1572864 | tf_op jit(solution)/shard_map/all_to_all | solution.py:39
  145.1 0.2 reduce-scatter.2.cloned.1.call-start
  145.4 11.8 %all-to-all-done.2 = bf16[32,128,4,24]{1,3,2,0:T(8,128)(2,1)S(1)} async-done(((bf16[32,128,4,24]{1,3,2,0:T(8,128)(2,1)}), bf16[32,128,4,24]{1,3,2,0:T(8,128)(2,1)S(1)}, u32[]{:S(2)}, u32[]{:S(2)}) %all-to-all-start.2) | async-done | bytes 786464 | tf_op jit(solution)/shard_map/all_to_all | solution.py:39
  157.2 0.3 convert_bitcast_fusion
  157.5 0.1 fusion.30
  157.6 0.3 broadcast_multiply_fusion
  157.9 0.2 copy.50
  158.2 0.3 broadcast_multiply_fusion.1
  158.5 0.2 copy.51
  158.7 0.3 broadcast_multiply_fusion.2
  159.1 0.2 copy.52
  159.3 0.3 broadcast_multiply_fusion.3
  159.6 0.2 copy.53
  159.9 13.6 %fusion.13 = bf16[16,24,2048]{2,1,0:T(8,128)(2,1)} fusion(bf16[4096,2048]{1,0:T(8,128)(2,1)} %all-gather.2.cloned.1.call-done, f32[24,4096]{1,0:T(8,128)S(1)} %bitcast.89, f32[24,4096]{1,0:T(8,128)S(1)} %bitcast.90, f32[24,4096]{1,0:T(8,128)S(1)} %bitcast.91, f32[24,4096]{1,0:T(8,128)S(1)} %bitcast.92, pred[16,4096]{1,0:T(8,128)(4,1)S(1)} %get-tuple-element.34, ...), kind=kOutput, calls=%fused_computation.18 | convolution fusion | flops 6455820288 | bytes 20185088 | tf_op jit(solution)/shard_map/dot_general | solution.py:48
  173.5 0.0 copy-start
  173.5 0.0 reduce-scatter.2.cloned.1.call-update
  173.5 1.1 copy-done
  174.6 0.1 pad_maximum_fusion
  174.7 2.5 copy.31
  177.2 69.0 %reduce-scatter.2.cloned.1.call-done = bf16[1,24,2048]{2,1,0:T(8,128)(2,1)} async-done(((bf16[16,24,2048]{2,1,0:T(8,128)(2,1)}), bf16[1,24,2048]{2,1,0:T(8,128)(2,1)}) %reduce-scatter.2.cloned.1.call-update) | async-done | bytes 98320 | tf_op jit(solution)/shard_map/reduce_scatter | solution.py:63
  246.2 1.6 multiply_convert_fusion
  (8 shorter events, 0.2 us)
Async XLA Ops:
  7.2 96.4 %all-gather.2.cloned.1.call-start = ((), (), s32[]{:S(2)}) async-start(), calls=%async_computation.4 | async-start | bytes 17301504 | tf_op jit(solution)/shard_map/all_gather | solution.py:18
  10.1 89.5 %all-to-all-start = ((bf16[16,1,24,2048]{3,2,1,0:T(8,128)(2,1)}), bf16[16,1,24,2048]{3,2,1,0:T(8,128)(2,1)}, u32[]{:S(2)}, u32[]{:S(2)}) async-start(bf16[16,1,24,2048]{3,2,1,0:T(8,128)(2,1)} %stack.12), calls=%async_computation | async-start | bytes 3145728 | tf_op jit(solution)/shard_map/all_to_all | solution.py:11
  27.3 1.4 copy-start.1
  27.3 24.5 %copy-start.2 = (s32[128,4]{0,1:T(4,128)S(1)}, s32[128,4]{0,1:T(4,128)}, u32[]{:S(2)}) copy-start(s32[128,4]{0,1:T(4,128)} %param.6) | copy-start | bytes 6148
  117.8 17.8 %all-to-all-start.1 = ((bf16[32,128,4,24]{1,3,2,0:T(8,128)(2,1)}), bf16[32,128,4,24]{1,3,2,0:T(8,128)(2,1)S(1)}, u32[]{:S(2)}, u32[]{:S(2)}) async-start(bf16[32,128,4,24]{1,3,2,0:T(8,128)(2,1)} %copy.25), calls=%async_computation.1 | async-start | bytes 1572864 | tf_op jit(solution)/shard_map/all_to_all | solution.py:55
  139.2 18.0 %all-to-all-start.2 = ((bf16[32,128,4,24]{1,3,2,0:T(8,128)(2,1)}), bf16[32,128,4,24]{1,3,2,0:T(8,128)(2,1)S(1)}, u32[]{:S(2)}, u32[]{:S(2)}) async-start(bf16[32,128,4,24]{1,3,2,0:T(8,128)(2,1)} %copy.29), calls=%async_computation.2 | async-start | bytes 1572864 | tf_op jit(solution)/shard_map/all_to_all | solution.py:39
  145.1 101.1 %reduce-scatter.2.cloned.1.call-start = ((), (), s32[]{:S(2)}) async-start(), calls=%async_computation.5 | async-start | bytes 1671168 | tf_op jit(solution)/shard_map/reduce_scatter | solution.py:63
  173.5 1.1 copy-start
Sparse Core Ops, SparseCore 0:
  11.1 92.4 all-gather.1
  173.6 72.4 reduce-scatter.1
